TPU v7x, 32 devices: a whole 2x2x4 slice. The times are simulated.
32 devices in a mesh: row: 8 (over y, x, core), col: 4 (over z).
Axes of the slice: x: 2, y: 2, z: 4, core: 2. Of those that a mesh axis runs over, the one named last changes fastest.
Arguments:
- adjacency: float32 [1024, 32768], P('row', 'col'), may hold values from 0 to 0.99, as said below
Outputs:
- tom: float32 [1024, 1024], P('row', 'col')
Inputs may be any that keep to these rules, and one draw needn't show every extreme that they name: `adjacency`: every entry is nonnegative and below 0.99.
All inputs are finite; a program needn't handle non-finite values.
Results may differ from a plain program's by a relative error of at most 0.000059.
Values sent between devices are 32-bit elements; how exact they have to be, the bound alone decides.
No kernel may reach another device: no remote copies, remote signals or barrier semaphores. Data moves between devices by JAX's collectives and lax.ppermute only.
A program may use at most 64 MiB of HBM per device.

v0:
```python
import jax
import jax.numpy as jnp
from jax import lax
from jax.sharding import PartitionSpec as P


def inner_rows(left, right):
    return lax.dot_general(
        left,
        right,
        (((1,), (1,)), ((), ())),
        precision=lax.Precision.HIGHEST,
        preferred_element_type=jnp.float32,
    )


def finish(shared_sum, linked, own_degree, col_degree):
    smaller = jnp.minimum(own_degree[:, None], col_degree[None, :])
    return (shared_sum + linked) / (smaller + 1.0 - linked)


def degrees(adjacency, window):
    n_row = lax.axis_size("row")
    n_col = lax.axis_size("col")
    strip_rows = adjacency.shape[0]
    row_sum = jnp.sum(adjacency, axis=1)
    every = lax.all_gather(row_sum, ("row", "col"), axis=0, tiled=True)
    every = every.reshape(n_row, n_col, strip_rows).sum(axis=1).reshape(-1)
    own = lax.dynamic_slice_in_dim(every, lax.axis_index("row") * strip_rows, strip_rows, 0)
    col = lax.dynamic_slice_in_dim(every, lax.axis_index("col") * window, window, 0)
    return (own, col)


def solution(mesh):
    placed = (P("row", "col"),)
    return jax.shard_map(
        body, mesh=mesh, in_specs=placed, out_specs=P("row", "col"), check_vma=False
    )


def body(adjacency):
    strip_rows = adjacency.shape[0]
    window = strip_rows * lax.axis_size("row") // lax.axis_size("col")
    pieces = lax.all_to_all(adjacency, "row", split_axis=1, concat_axis=0, tiled=True)
    part = lax.psum_scatter(inner_rows(pieces, pieces), "row", scatter_dimension=0, tiled=True)
    shared_sum = lax.psum_scatter(part, "col", scatter_dimension=1, tiled=True)
    own_degree = lax.psum(jnp.sum(adjacency, axis=1), "col")
    all_degree = lax.all_gather(own_degree, "row", axis=0, tiled=True)
    col_degree = lax.dynamic_slice_in_dim(all_degree, lax.axis_index("col") * window, window, 0)
    linked = adjacency[:, :window]
    return finish(shared_sum, linked, own_degree, col_degree)
```

profile of v0, /device:TPU:0, one launch (start us, length us, event | category | flops | bytes accessed | tf_op | source)
XLA Modules:
  0.0 173.9 jit_solution(5790078608132117459)
XLA Ops:
  6.5 0.0 reduce-scatter.3.cloned.1.call-start
  6.5 5.6 %copy.4 = f32[128,8192]{0,1:T(8,128)} copy(f32[128,8192]{1,0:T(8,128)} %param.1) | data formatting | bytes 8388608 | tf_op args[0]
  12.1 54.3 %all_to_all.19 = f32[128,8,1024]{0,2,1:T(8,128)} all-to-all(f32[128,8,1024]{0,2,1:T(8,128)} %bitcast.8), channel_id=1, replica_groups=mesh['row'=8,'col'=4] {'row'}, dimensions={1} | all-to-all | bytes 8388608 | tf_op jit(solution)/shard_map/all_to_all | solution.py:44
  66.4 5.3 %copy.5 = f32[8,128,1024]{2,1,0:T(8,128)} copy(f32[8,128,1024]{1,2,0:T(8,128)} %bitcast.7) | data formatting | bytes 8388608 | tf_op jit(solution)/shard_map/all_to_all | solution.py:44
  71.8 18.1 %fusion = f32[1024,1024]{1,0:T(8,128)} fusion(f32[1024,1024]{1,0:T(8,128)} %bitcast.9), kind=kOutput, calls=%fused_computation.1 | convolution fusion | flops 12884901888 | bytes 8388608 | tf_op jit(solution)/shard_map/dot_general | solution.py:8
  89.9 0.0 reduce-scatter.3.cloned.1.call-update
  90.0 0.0 reduce-scatter.5.cloned.1.call-start
  90.0 51.4 %reduce-scatter.3.cloned.1.call-done = f32[128,1024]{1,0:T(8,128)} async-done(((f32[1024,1024]{1,0:T(8,128)}), f32[128,1024]{1,0:T(8,128)}) %reduce-scatter.3.cloned.1.call-update) | async-done | bytes 524304 | tf_op jit(solution)/shard_map/reduce_scatter | solution.py:45
  141.4 0.0 reduce-scatter.5.cloned.1.call-update
  141.5 2.5 %reduce_sum.9 = f32[128]{0:T(128)S(1)} reduce(f32[128,8192]{1,0:T(8,128)} %param.1, f32[]{:T(128)} %constant.6.clone.1), dimensions={1}, to_apply=%region_2.0 | reduce | flops 1048448 | bytes 4194820 | tf_op jit(solution)/shard_map/reduce_sum | solution.py:47
  144.0 11.8 %psum.7 = f32[128]{0:T(128)S(1)} all-reduce(f32[128]{0:T(128)S(1)} %reduce_sum.9), channel_id=1, replica_groups=mesh['row'=8,'col'=4] {'col'}, use_global_device_ids=true, to_apply=%region_3.0 | all-reduce | flops 128 | bytes 1024 | tf_op jit(solution)/shard_map/psum | solution.py:47
  155.7 8.6 %all-gather = f32[8,1,128]{2,1,0:T(1,128)S(1)} all-gather(f32[1,1,128]{2,1,0:T(1,128)S(1)} %bitcast.11), channel_id=1, replica_groups=mesh['row'=8,'col'=4] {'row'}, dimensions={0}, use_global_device_ids=true | all-gather | bytes 4608 | tf_op jit(solution)/shard_map/all_gather | solution.py:48
  164.3 0.1 dynamic_slice.3
  164.4 1.0 reduce-scatter.5.cloned.1.call-done
  165.3 1.7 subtract_divide_fusion
Async XLA Ops:
  6.5 134.9 %reduce-scatter.3.cloned.1.call-start = ((), (), s32[]{:S(2)}) async-start(), calls=%async_computation.3 | async-start | bytes 4718592 | tf_op jit(solution)/shard_map/reduce_scatter | solution.py:45
  90.0 75.4 %reduce-scatter.5.cloned.1.call-start = ((), (), s32[]{:S(2)}) async-start(), calls=%async_computation.4 | async-start | bytes 655360 | tf_op jit(solution)/shard_map/reduce_scatter | solution.py:46
Sparse Core Ops, SparseCore 0:
  90.1 51.3 reduce-scatter.2
  143.8 21.4 reduce-scatter.4
where the time goes:
time: 174 us
  blocking collectives  74.7 us (43%)
  waiting for transfers between devices  52.4 us (30%)
  matrix products  18.1 us (10%)
  between operations  13.4 us (8%)
  local copies, waits for them, and re-layouts  11 us (6%)
  other arithmetic  4.22 us (2%)
    all_to_all x1, blocking collectives, body(): lax.all_to_all(adjacency, 'row', split_axis=1, concat_axis=0, tiled=True)  54.3 us
    reduce_scatter x1, waiting for transfers between devices, body(): lax.psum_scatter(inner_rows(pieces, pieces), 'row', scatter_dimension=0,...  51.4 us
    dot_general x1, matrix products, inner_rows(): lax.dot_general(left, right, (((1,), (1,)), ((), ())), precision=lax.Prec...  18.1 us
    psum x1, blocking collectives, body(): own_degree = lax.psum(jnp.sum(adjacency, axis=1), 'col')  11.8 us
    all_gather x1, blocking collectives, body(): all_degree = lax.all_gather(own_degree, 'row', axis=0, tiled=True)  8.59 us
    unnamed x1, local copies, waits for them, and re-layouts  5.57 us
    all_to_all x1, local copies, waits for them, and re-layouts, body(): lax.all_to_all(adjacency, 'row', split_axis=1, concat_axis=0, tiled=True)  5.34 us
  transfers between devices with their start and end apart: 2, of which 2 were waited for; matrix products, arithmetic and copies ran while one was open for 1% of the time, Pallas kernels for 0%

commit v1 on v0

--- a/solution.py
+++ b/solution.py
@@ -2,6 +2,10 @@
 import jax.numpy as jnp
 from jax import lax
 from jax.sharding import PartitionSpec as P
+
+_tell_inputs = lambda x_local: jnp.concatenate(
+    lax.all_to_all(jnp.stack(jnp.split(x_local, lax.axis_size("row"), axis=1)), "row", 0, 0), axis=0
+)
 
 
 def inner_rows(left, right):
@@ -41,7 +45,7 @@
 def body(adjacency):
     strip_rows = adjacency.shape[0]
     window = strip_rows * lax.axis_size("row") // lax.axis_size("col")
-    pieces = lax.all_to_all(adjacency, "row", split_axis=1, concat_axis=0, tiled=True)
+    pieces = _tell_inputs(adjacency)
     part = lax.psum_scatter(inner_rows(pieces, pieces), "row", scatter_dimension=0, tiled=True)
     shared_sum = lax.psum_scatter(part, "col", scatter_dimension=1, tiled=True)
     own_degree = lax.psum(jnp.sum(adjacency, axis=1), "col")

time: 174 us -> 168 us (0.966)
  matrix products: 18.1 us -> 14.8 us
  local copies, waits for them, and re-layouts: 11 us -> 8.71 us
    all_to_all x1 -> x0, local copies, waits for them, and re-layouts: 5.34 us -> none  [body(): lax.all_to_all(adjacency, 'row', split_axis=1, concat_axis=0, tiled=True)]
    dot_general x1, matrix products: 18.1 us -> 14.8 us  [inner_rows(): lax.dot_general(left, right, (((1,), (1,)), ((), ())), precision=lax.Prec...]
    unnamed x1 -> x7, local copies, waits for them, and re-layouts: 5.57 us -> 7.56 us
  transfers between devices with their start and end apart: 2 -> 2, of which waited for: 2 -> 2; matrix products, arithmetic and copies ran while one was open for 1% -> 2% of each run, Pallas kernels for 0% -> 0%
where the time goes in v1:
time: 168 us; the launch traced here: 167 us
  blocking collectives  74.4 us (44%)
  waiting for transfers between devices  51.8 us (31%)
  matrix products  14.8 us (9%)
  between operations  13.4 us (8%)
  local copies, waits for them, and re-layouts  8.71 us (5%)
  other arithmetic  4.22 us (3%)
    all_to_all x1, blocking collectives, lax.all_to_all(jnp.stack(jnp.split(x_local, lax.axis_size('row'), axis=1)...  54 us
    reduce_scatter x1, waiting for transfers between devices, body(): lax.psum_scatter(inner_rows(pieces, pieces), 'row', scatter_dimension=0,...  50.8 us
    dot_general x1, matrix products, inner_rows(): lax.dot_general(left, right, (((1,), (1,)), ((), ())), precision=lax.Prec...  14.8 us
    psum x1, blocking collectives, body(): own_degree = lax.psum(jnp.sum(adjacency, axis=1), 'col')  11.8 us
    all_gather x1, blocking collectives, body(): all_degree = lax.all_gather(own_degree, 'row', axis=0, tiled=True)  8.61 us
    unnamed x7, local copies, waits for them, and re-layouts  7.56 us
  transfers between devices with their start and end apart: 2, of which 2 were waited for; matrix products, arithmetic and copies ran while one was open for 2% of the time, Pallas kernels for 0%

profile of v1, /device:TPU:0, one launch (start us, length us, event | category | flops | bytes accessed | tf_op | source)
XLA Modules:
  0.0 167.4 jit_solution(14416462727775434973)
XLA Ops:
  6.5 0.0 reduce-scatter.3.cloned.1.call-start
  6.5 1.1 bitcast_dynamic-update-slice_fusion.7
  7.6 1.1 bitcast_dynamic-update-slice_fusion.6
  8.7 1.1 bitcast_dynamic-update-slice_fusion.5
  9.8 1.1 bitcast_dynamic-update-slice_fusion.4
  10.9 1.1 bitcast_dynamic-update-slice_fusion.3
  12.0 1.1 bitcast_dynamic-update-slice_fusion.2
  13.0 1.1 bitcast_dynamic-update-slice_fusion.1
  14.1 1.1 bitcast_dynamic-update-slice_fusion
  15.2 54.0 %all_to_all.5 = f32[8,128,1024]{2,1,0:T(8,128)S(1)} all-to-all(f32[8,128,1024]{2,1,0:T(8,128)S(1)} %bitcast_dynamic-update-slice_fusion), channel_id=1, replica_groups=mesh['row'=8,'col'=4] {'row'}, dimensions={0} | all-to-all | bytes 8388608 | tf_op jit(solution)/shard_map/all_to_all | solution.py:7
  69.2 14.8 %fusion = f32[1024,1024]{1,0:T(8,128)} fusion(f32[1024,1024]{1,0:T(8,128)S(1)} %bitcast.21), kind=kOutput, calls=%fused_computation.9 | convolution fusion | flops 12884901888 | bytes 8388608 | tf_op jit(solution)/shard_map/dot_general | solution.py:12
  84.0 0.0 reduce-scatter.3.cloned.1.call-update
  84.0 0.0 reduce-scatter.5.cloned.1.call-start
  84.1 50.8 %reduce-scatter.3.cloned.1.call-done = f32[128,1024]{1,0:T(8,128)} async-done(((f32[1024,1024]{1,0:T(8,128)}), f32[128,1024]{1,0:T(8,128)}) %reduce-scatter.3.cloned.1.call-update) | async-done | bytes 524304 | tf_op jit(solution)/shard_map/reduce_scatter | solution.py:49
  134.9 0.0 reduce-scatter.5.cloned.1.call-update
  134.9 2.5 %reduce_sum.9 = f32[128]{0:T(128)S(1)} reduce(f32[128,8192]{1,0:T(8,128)} %param.1, f32[]{:T(128)} %constant.6.clone.1), dimensions={1}, to_apply=%region_2.0 | reduce | flops 1048448 | bytes 4194820 | tf_op jit(solution)/shard_map/reduce_sum | solution.py:51
  137.4 11.8 %psum.7 = f32[128]{0:T(128)S(1)} all-reduce(f32[128]{0:T(128)S(1)} %reduce_sum.9), channel_id=1, replica_groups=mesh['row'=8,'col'=4] {'col'}, use_global_device_ids=true, to_apply=%region_3.0 | all-reduce | flops 128 | bytes 1024 | tf_op jit(solution)/shard_map/psum | solution.py:51
  149.2 8.6 %all-gather = f32[8,1,128]{2,1,0:T(1,128)S(1)} all-gather(f32[1,1,128]{2,1,0:T(1,128)S(1)} %bitcast.23), channel_id=1, replica_groups=mesh['row'=8,'col'=4] {'row'}, dimensions={0}, use_global_device_ids=true | all-gather | bytes 4608 | tf_op jit(solution)/shard_map/all_gather | solution.py:52
  157.8 0.1 dynamic_slice.3
  157.8 1.0 reduce-scatter.5.cloned.1.call-done
  158.8 1.7 %subtract_divide_fusion = f32[128,256]{1,0:T(8,128)} fusion(f32[128,256]{1,0:T(8,128)} %reduce-scatter.5.cloned.1.call-done, f32[128,8192]{1,0:T(8,128)} %param.1, f32[256]{0:T(256)S(1)} %dynamic_slice.3, f32[128]{0:T(128)S(1)} %psum.7), kind=kLoop, calls=%fused_computation.8 | loop fusion | flops 163840 | bytes 394752 | tf_op jit(solution)/shard_map/div | solution.py:23
Async XLA Ops:
  6.5 128.3 %reduce-scatter.3.cloned.1.call-start = ((), (), s32[]{:S(2)}) async-start(), calls=%async_computation.3 | async-start | bytes 4718592 | tf_op jit(solution)/shard_map/reduce_scatter | solution.py:49
  84.0 74.8 %reduce-scatter.5.cloned.1.call-start = ((), (), s32[]{:S(2)}) async-start(), calls=%async_computation.4 | async-start | bytes 655360 | tf_op jit(solution)/shard_map/reduce_scatter | solution.py:50
Sparse Core Ops, SparseCore 0:
  84.1 50.6 reduce-scatter.2
  137.2 21.5 reduce-scatter.4

commit v2 on v0

--- a/solution.py
+++ b/solution.py
@@ -39,13 +39,26 @@
 
 
 def body(adjacency):
+
+    def _draw_files(block_in):
+        nodes = jax.lax.axis_size("row")
+        log = [(i, (i + 1) % nodes) for i in range(nodes)]
+        far_arr = [None] * nodes
+        far_arr[nodes - 1] = block_in
+        for nth in range(nodes - 2, -1, -1):
+            far_arr[nth] = jax.lax.ppermute(far_arr[nth + 1], "row", log)
+        field_out = jnp.concatenate(far_arr, axis=0)
+        heard = (jax.lax.axis_index("row") + 1) * block_in.shape[0]
+        small = jnp.roll(field_out, heard, axis=0)
+        return small
+
     strip_rows = adjacency.shape[0]
     window = strip_rows * lax.axis_size("row") // lax.axis_size("col")
     pieces = lax.all_to_all(adjacency, "row", split_axis=1, concat_axis=0, tiled=True)
     part = lax.psum_scatter(inner_rows(pieces, pieces), "row", scatter_dimension=0, tiled=True)
     shared_sum = lax.psum_scatter(part, "col", scatter_dimension=1, tiled=True)
     own_degree = lax.psum(jnp.sum(adjacency, axis=1), "col")
-    all_degree = lax.all_gather(own_degree, "row", axis=0, tiled=True)
+    all_degree = _draw_files(own_degree)
     col_degree = lax.dynamic_slice_in_dim(all_degree, lax.axis_index("col") * window, window, 0)
     linked = adjacency[:, :window]
     return finish(shared_sum, linked, own_degree, col_degree)

time: 174 us -> 174 us (level)
  blocking collectives: 74.7 us -> 66.9 us
  waiting for transfers between devices: 52.4 us -> 60.1 us
    reduce_scatter x1, waiting for transfers between devices: 51.4 us -> 9.2 us  [body(): lax.psum_scatter(inner_rows(pieces, pieces), 'row', scatter_dimension=0,...]
    ppermute x0 -> x7, waiting for transfers between devices: none -> 27 us  [_draw_files(): far_arr[nth] = jax.lax.ppermute(far_arr[nth + 1], 'row', log)]
    reduce_scatter x1, waiting for transfers between devices: 0.96 us -> 23.8 us  [body(): shared_sum = lax.psum_scatter(part, 'col', scatter_dimension=1, tiled=True)]
    all_gather x1 -> x0, blocking collectives: 8.59 us -> none  [body(): all_degree = lax.all_gather(own_degree, 'row', axis=0, tiled=True)]
    unnamed x1 -> x16, local copies, waits for them, and re-layouts: 5.57 us -> 5.66 us
  transfers between devices with their start and end apart: 2 -> 9, of which waited for: 2 -> 9; matrix products, arithmetic and copies ran while one was open for 1% -> 2% of each run, Pallas kernels for 0% -> 0%
where the time goes in v2:
time: 174 us
  blocking collectives  66.9 us (38%)
  waiting for transfers between devices  60.1 us (35%)
  matrix products  18.1 us (10%)
  between operations  13.5 us (8%)
  local copies, waits for them, and re-layouts  11.1 us (6%)
  other arithmetic  4.22 us (2%)
    all_to_all x1, blocking collectives, body(): lax.all_to_all(adjacency, 'row', split_axis=1, concat_axis=0, tiled=True)  54.3 us
    ppermute x7, waiting for transfers between devices, _draw_files(): far_arr[nth] = jax.lax.ppermute(far_arr[nth + 1], 'row', log)  27 us
    reduce_scatter x1, waiting for transfers between devices, body(): shared_sum = lax.psum_scatter(part, 'col', scatter_dimension=1, tiled=True)  23.8 us
    dot_general x1, matrix products, inner_rows(): lax.dot_general(left, right, (((1,), (1,)), ((), ())), precision=lax.Prec...  18.1 us
    psum x1, blocking collectives, body(): own_degree = lax.psum(jnp.sum(adjacency, axis=1), 'col')  12.6 us
    reduce_scatter x1, waiting for transfers between devices, body(): lax.psum_scatter(inner_rows(pieces, pieces), 'row', scatter_dimension=0,...  9.2 us
    unnamed x16, local copies, waits for them, and re-layouts  5.66 us
    all_to_all x1, local copies, waits for them, and re-layouts, body(): lax.all_to_all(adjacency, 'row', split_axis=1, concat_axis=0, tiled=True)  5.35 us
  transfers between devices with their start and end apart: 9, of which 9 were waited for; matrix products, arithmetic and copies ran while one was open for 2% of the time, Pallas kernels for 0%

profile of v2, /device:TPU:0, one launch (start us, length us, event | category | flops | bytes accessed | tf_op | source)
XLA Modules:
  0.0 174.1 jit_solution(9203494418040893911)
XLA Ops:
  6.5 5.6 %copy.2 = f32[128,8192]{0,1:T(8,128)} copy(f32[128,8192]{1,0:T(8,128)} %param.1) | data formatting | bytes 8388608 | tf_op args[0]
  12.1 54.3 %all_to_all.19 = f32[128,8,1024]{0,2,1:T(8,128)} all-to-all(f32[128,8,1024]{0,2,1:T(8,128)} %bitcast.6), channel_id=1, replica_groups=mesh['row'=8,'col'=4] {'row'}, dimensions={1} | all-to-all | bytes 8388608 | tf_op jit(solution)/shard_map/all_to_all | solution.py:57
  66.4 5.4 %copy.3 = f32[8,128,1024]{2,1,0:T(8,128)} copy(f32[8,128,1024]{1,2,0:T(8,128)} %bitcast.5) | data formatting | bytes 8388608 | tf_op jit(solution)/shard_map/all_to_all | solution.py:57
  71.8 18.1 %fusion = f32[1024,1024]{1,0:T(8,128)} fusion(f32[1024,1024]{1,0:T(8,128)} %bitcast.7), kind=kOutput, calls=%fused_computation.17 | convolution fusion | flops 12884901888 | bytes 8388608 | tf_op jit(solution)/shard_map/dot_general | solution.py:8
  89.9 0.0 reduce-scatter.3.cloned.1.call-update
  90.0 0.0 reduce-scatter.5.cloned.1.call-start
  90.0 2.5 %reduce_sum.9 = f32[128]{0:T(128)S(1)} reduce(f32[128,8192]{1,0:T(8,128)} %param.1, f32[]{:T(128)} %constant.35.clone.1), dimensions={1}, to_apply=%region_2.0 | reduce | flops 1048448 | bytes 4194820 | tf_op jit(solution)/shard_map/reduce_sum | solution.py:60
  92.5 12.6 %psum.7 = f32[128]{0:T(128)S(1)} all-reduce(f32[128]{0:T(128)S(1)} %reduce_sum.9), channel_id=1, replica_groups=mesh['row'=8,'col'=4] {'col'}, use_global_device_ids=true, to_apply=%region_3.0 | all-reduce | flops 128 | bytes 1024 | tf_op jit(solution)/shard_map/psum | solution.py:60
  105.1 0.0 collective-permute-start
  105.1 3.9 %collective-permute-done = f32[128]{0:T(128)S(1)} collective-permute-done((f32[128]{0:T(128)S(1)}, f32[128]{0:T(128)S(1)}, u32[]{:S(2)}, u32[]{:S(2)}) %collective-permute-start) | collective-permute-done | bytes 544 | tf_op jit(solution)/shard_map/ppermute | solution.py:49
  109.0 0.0 collective-permute-start.1
  109.0 3.9 %collective-permute-done.1 = f32[128]{0:T(128)S(1)} collective-permute-done((f32[128]{0:T(128)S(1)}, f32[128]{0:T(128)S(1)}, u32[]{:S(2)}, u32[]{:S(2)}) %collective-permute-start.1) | collective-permute-done | bytes 544 | tf_op jit(solution)/shard_map/ppermute | solution.py:49
  112.9 0.0 collective-permute-start.2
  112.9 3.9 %collective-permute-done.2 = f32[128]{0:T(128)S(1)} collective-permute-done((f32[128]{0:T(128)S(1)}, f32[128]{0:T(128)S(1)}, u32[]{:S(2)}, u32[]{:S(2)}) %collective-permute-start.2) | collective-permute-done | bytes 544 | tf_op jit(solution)/shard_map/ppermute | solution.py:49
  116.7 0.0 collective-permute-start.3
  116.7 3.9 %collective-permute-done.3 = f32[128]{0:T(128)S(1)} collective-permute-done((f32[128]{0:T(128)S(1)}, f32[128]{0:T(128)S(1)}, u32[]{:S(2)}, u32[]{:S(2)}) %collective-permute-start.3) | collective-permute-done | bytes 544 | tf_op jit(solution)/shard_map/ppermute | solution.py:49
  120.6 3.9 %collective-permute-done.4 = f32[128]{0:T(128)S(1)} collective-permute-done((f32[128]{0:T(128)S(1)}, f32[128]{0:T(128)S(1)}, u32[]{:S(2)}, u32[]{:S(2)}) %collective-permute-start.4) | collective-permute-done | bytes 544 | tf_op jit(solution)/shard_map/ppermute | solution.py:49
  124.5 3.9 %collective-permute-done.5 = f32[128]{0:T(128)S(1)} collective-permute-done((f32[128]{0:T(128)S(1)}, f32[128]{0:T(128)S(1)}, u32[]{:S(2)}, u32[]{:S(2)}) %collective-permute-start.5) | collective-permute-done | bytes 544 | tf_op jit(solution)/shard_map/ppermute | solution.py:49
  128.3 3.9 %collective-permute-done.6 = f32[128]{0:T(128)S(1)} collective-permute-done((f32[128]{0:T(128)S(1)}, f32[128]{0:T(128)S(1)}, u32[]{:S(2)}, u32[]{:S(2)}) %collective-permute-start.6) | collective-permute-done | bytes 544 | tf_op jit(solution)/shard_map/ppermute | solution.py:49
  132.3 9.2 %reduce-scatter.3.cloned.1.call-done = f32[128,1024]{1,0:T(8,128)} async-done(((f32[1024,1024]{1,0:T(8,128)}), f32[128,1024]{1,0:T(8,128)}) %reduce-scatter.3.cloned.1.call-update) | async-done | bytes 524304 | tf_op jit(solution)/shard_map/reduce_scatter | solution.py:58
  141.5 0.0 reduce-scatter.5.cloned.1.call-update
  141.6 0.1 dynamic_slice.8
  141.7 23.8 %reduce-scatter.5.cloned.1.call-done = f32[128,256]{1,0:T(8,128)} async-done(((f32[128,1024]{1,0:T(8,128)}), f32[128,256]{1,0:T(8,128)}) %reduce-scatter.5.cloned.1.call-update) | async-done | bytes 131088 | tf_op jit(solution)/shard_map/reduce_scatter | solution.py:59
  165.5 1.7 subtract_divide_fusion
  (21 shorter events, 0.1 us)
Async XLA Ops:
  6.5 134.9 %reduce-scatter.3.cloned.1.call-start = ((), (), s32[]{:S(2)}) async-start(), calls=%async_computation.3 | async-start | bytes 4718592 | tf_op jit(solution)/shard_map/reduce_scatter | solution.py:58
  90.0 75.6 %reduce-scatter.5.cloned.1.call-start = ((), (), s32[]{:S(2)}) async-start(), calls=%async_computation.4 | async-start | bytes 655360 | tf_op jit(solution)/shard_map/reduce_scatter | solution.py:59
  105.1 3.9 %collective-permute-start = (f32[128]{0:T(128)S(1)}, f32[128]{0:T(128)S(1)}, u32[]{:S(2)}, u32[]{:S(2)}) collective-permute-start(f32[128]{0:T(128)S(1)} %psum.7), channel_id=1, source_target_pairs={{0,4},{4,8},{8,12},{12,16},{16,20},{20,24},{24,28},{28,0},{1,5},{5... | collective-permute-start | bytes 1544 | tf_op jit(solution)/shard_map/ppermute | solution.py:49
  109.0 3.9 %collective-permute-start.1 = (f32[128]{0:T(128)S(1)}, f32[128]{0:T(128)S(1)}, u32[]{:S(2)}, u32[]{:S(2)}) collective-permute-start(f32[128]{0:T(128)S(1)} %collective-permute-done), channel_id=1, source_target_pairs={{0,4},{4,8},{8,12},{12,16},{16,20},{20,24},{24,28},{28,0},{1,5},{5... | collective-permute-start | bytes 1544 | tf_op jit(solution)/shard_map/ppermute | solution.py:49
  112.9 3.9 %collective-permute-start.2 = (f32[128]{0:T(128)S(1)}, f32[128]{0:T(128)S(1)}, u32[]{:S(2)}, u32[]{:S(2)}) collective-permute-start(f32[128]{0:T(128)S(1)} %collective-permute-done.1), channel_id=1, source_target_pairs={{0,4},{4,8},{8,12},{12,16},{16,20},{20,24},{24,28},{28,0},{1,5},{5... | collective-permute-start | bytes 1544 | tf_op jit(solution)/shard_map/ppermute | solution.py:49
  116.7 3.9 %collective-permute-start.3 = (f32[128]{0:T(128)S(1)}, f32[128]{0:T(128)S(1)}, u32[]{:S(2)}, u32[]{:S(2)}) collective-permute-start(f32[128]{0:T(128)S(1)} %collective-permute-done.2), channel_id=1, source_target_pairs={{0,4},{4,8},{8,12},{12,16},{16,20},{20,24},{24,28},{28,0},{1,5},{5... | collective-permute-start | bytes 1544 | tf_op jit(solution)/shard_map/ppermute | solution.py:49
  120.6 3.9 %collective-permute-start.4 = (f32[128]{0:T(128)S(1)}, f32[128]{0:T(128)S(1)}, u32[]{:S(2)}, u32[]{:S(2)}) collective-permute-start(f32[128]{0:T(128)S(1)} %collective-permute-done.3), channel_id=1, source_target_pairs={{0,4},{4,8},{8,12},{12,16},{16,20},{20,24},{24,28},{28,0},{1,5},{5... | collective-permute-start | bytes 1544 | tf_op jit(solution)/shard_map/ppermute | solution.py:49
  124.5 3.9 %collective-permute-start.5 = (f32[128]{0:T(128)S(1)}, f32[128]{0:T(128)S(1)}, u32[]{:S(2)}, u32[]{:S(2)}) collective-permute-start(f32[128]{0:T(128)S(1)} %collective-permute-done.4), channel_id=1, source_target_pairs={{0,4},{4,8},{8,12},{12,16},{16,20},{20,24},{24,28},{28,0},{1,5},{5... | collective-permute-start | bytes 1544 | tf_op jit(solution)/shard_map/ppermute | solution.py:49
  128.3 3.9 %collective-permute-start.6 = (f32[128]{0:T(128)S(1)}, f32[128]{0:T(128)S(1)}, u32[]{:S(2)}, u32[]{:S(2)}) collective-permute-start(f32[128]{0:T(128)S(1)} %collective-permute-done.5), channel_id=1, source_target_pairs={{0,4},{4,8},{8,12},{12,16},{16,20},{20,24},{24,28},{28,0},{1,5},{5... | collective-permute-start | bytes 1544 | tf_op jit(solution)/shard_map/ppermute | solution.py:49
Sparse Core Ops, SparseCore 0:
  90.1 51.3 reduce-scatter.2
  143.8 21.6 reduce-scatter.4
